TPU v7x, 256 devices: a whole 4x4x8 slice. The times are simulated.
256 devices in a mesh: blk: 32 (over x, y, core), sub: 8 (over z).
Axes of the slice: x: 4, y: 4, z: 8, core: 2. Of those that a mesh axis runs over, the one named last changes fastest.
Arguments:
- block_vec: bfloat16 [64, 512, 512], P('blk', 'sub'), may hold values from -6 to 6
- left_factor: bfloat16 [8, 512, 512], replicated, may hold values from -0.25 to 0.25
- right_factor: bfloat16 [8, 512, 512], replicated, may hold values from -0.25 to 0.25
- pairs: int32 [32, 32, 2, 3], replicated, may hold values from 0 to 7, as said below
- pair_count: int32 [32, 32], replicated, may hold values from 1 to 2, as said below
- left_basis: bfloat16 [64, 512, 512], P('blk'), may hold values from -0.25 to 0.25
- left_dual: bfloat16 [64, 512, 512], P('blk'), may hold values from -0.25 to 0.25
- right_eigenvector_matrix: bfloat16 [64, 512, 512], P('blk'), may hold values from -0.25 to 0.25
- right_dual: bfloat16 [64, 512, 512], P('blk'), may hold values from -0.25 to 0.25
- left_rates: float32 [64, 512], P('blk', 'sub'), may hold values from 0.5 to 8
- right_rates: float32 [64, 512], P('blk'), may hold values from 0.5 to 8
Outputs:
- next_vec: float32 [64, 512, 512], P('blk', None, 'sub')
Inputs may be any that keep to these rules, and one draw needn't show every extreme that they name: `pairs`: entry [g, h, c, 0] is a source block index within group g, [g, h, c, 1] a target block index within group h (0 to 1), and [g, h, c, 2] a term index (0 to 7); where g equals h, source and target differ. For some target group h, pair_count[g, h] is 2 for every g.
All inputs are finite; a program needn't handle non-finite values.
Results may differ from a plain program's by a relative error of at most 0.023.
Values may be sent and summed in bfloat16 or wider, within the bound.
No kernel may reach another device: no remote copies, remote signals or barrier semaphores. Data moves between devices by JAX's collectives and lax.ppermute only.
A program may use at most 64 MiB of HBM per device.

v0:
```python
import jax
import jax.numpy as jnp
from jax import lax
from jax.sharding import PartitionSpec as P


def local(
    block_vec,
    left_factor,
    right_factor,
    pairs,
    pair_count,
    left_basis,
    left_dual,
    right_eigenvector_matrix,
    right_dual,
    left_rates,
    right_rates,
):
    owner = lax.axis_index("blk")
    groups = lax.axis_size("blk")
    local_blocks = block_vec.shape[0]
    row_count = block_vec.shape[1]
    width_two = block_vec.shape[2]
    slots_per = pairs.shape[2]
    term_total = left_factor.shape[0]
    all_count = groups * local_blocks
    incoming = lax.dynamic_index_in_dim(pairs, owner, 1, keepdims=False)
    counts = lax.dynamic_index_in_dim(pair_count, owner, 1, keepdims=False)
    live_mask = (jnp.arange(slots_per)[None, :] < counts[:, None]).astype(jnp.float32)
    target_term = incoming[..., 1] * term_total + incoming[..., 2]
    source = jnp.arange(groups, dtype=jnp.int32)[:, None] * local_blocks + incoming[..., 0]
    key_onehot = (
        target_term[..., None] == jnp.arange(local_blocks * term_total)[None, None, :]
    ).astype(jnp.float32) * live_mask[..., None]
    source_onehot = (source[..., None] == jnp.arange(all_count)[None, None, :]).astype(jnp.float32)
    weights = jnp.einsum("gqk,gqs->ks", key_onehot, source_onehot).astype(jnp.bfloat16)
    everything = lax.all_gather(block_vec, "blk", axis=0, tiled=True)
    pooled = jnp.einsum(
        "ks,srn->krn", weights, everything, preferred_element_type=jnp.float32
    ).astype(jnp.bfloat16)
    pooled = pooled.reshape(local_blocks, term_total, row_count, width_two)
    right_done = jnp.einsum(
        "ktrn,tmn->ktrm", pooled, right_factor, preferred_element_type=jnp.float32
    ).astype(jnp.bfloat16)
    right_cols = lax.all_to_all(right_done, "sub", split_axis=3, concat_axis=2, tiled=True)
    summed = jnp.einsum(
        "tab,ktbc->kac", left_factor, right_cols, preferred_element_type=jnp.float32
    ).astype(jnp.bfloat16)
    dual_cols = jnp.einsum(
        "jab,jbc->jac", left_dual, summed, preferred_element_type=jnp.float32
    ).astype(jnp.bfloat16)
    dual_rows = lax.all_to_all(dual_cols, "sub", split_axis=1, concat_axis=2, tiled=True)
    mixed = jnp.einsum("jrn,jmn->jrm", dual_rows, right_dual, preferred_element_type=jnp.float32)
    scaled = (mixed / (left_rates[:, :, None] + right_rates[:, None, :])).astype(jnp.bfloat16)
    basis_rows = jnp.einsum(
        "jrm,jkm->jrk", scaled, right_eigenvector_matrix, preferred_element_type=jnp.float32
    ).astype(jnp.bfloat16)
    basis_cols = lax.all_to_all(basis_rows, "sub", split_axis=2, concat_axis=1, tiled=True)
    return jnp.einsum("jab,jbc->jac", left_basis, basis_cols, preferred_element_type=jnp.float32)


def solution(mesh):
    placed = (
        P("blk", "sub", None),
        P(),
        P(),
        P(),
        P(),
        P("blk", None, None),
        P("blk", None, None),
        P("blk", None, None),
        P("blk", None, None),
        P("blk", "sub"),
        P("blk", None),
    )
    return jax.shard_map(
        local, mesh=mesh, in_specs=placed, out_specs=P("blk", None, "sub"), check_vma=False
    )
```

profile of v0, /device:TPU:2, one launch (start us, length us, event | category | flops | bytes accessed | tf_op | source)
XLA Modules:
  0.0 167.2 jit_solution(14784271772205998171)
XLA Ops:
  6.5 0.7 all-gather.2.cloned.1.call-update
  7.3 1.1 constant_dynamic-slice_fusion
  8.3 0.1 copy.25
  8.4 0.9 dynamic-slice_reduce_fusion
  9.4 54.3 %all-gather.2.cloned.1.call-done = bf16[64,64,512]{2,1,0:T(8,128)(2,1)} async-done(((bf16[2,64,512]{2,1,0:T(8,128)(2,1)}), bf16[64,64,512]{2,1,0:T(8,128)(2,1)}) %all-gather.2.cloned.1.call-update) | async-done | bytes 4194320 | tf_op jit(solution)/shard_map/all_gather | solution.py:38
  63.7 6.7 %fusion.15 = bf16[2,8,64,512]{3,1,0,2:T(8,128)(2,1)S(1)} fusion(bf16[64,64,512]{2,1,0:T(8,128)(2,1)} %all-gather.2.cloned.1.call-done, s32[32,2]{0,1:T(2,128)S(1)} %get-tuple-element.6, bf16[32,2]{0,1:T(2,128)(2,1)S(1)} %compare_convert_fusion, s32[32,2]{0,1:T(2,128)S(1)} %get-tuple-element.5), kind=kOutput, calls=%fused_computation.10 | convolution fusion | flops 67770368 | bytes 5243520 | tf_op jit(solution)/shard_map/ks,srn->krn/dot_general | solution.py:39
  70.4 4.8 %fusion.12 = bf16[2,8,64,512]{3,2,0,1:T(8,128)(2,1)} fusion(bf16[8,512,512]{2,1,0:T(8,128)(2,1)} %param.13, bf16[2,8,64,512]{3,1,0,2:T(8,128)(2,1)S(1)} %fusion.15), kind=kOutput, calls=%fused_computation.9 | convolution fusion | flops 537395200 | bytes 6291456 | tf_op jit(solution)/shard_map/ktrn,tmn->ktrm/dot_general | solution.py:43
  75.2 4.7 %copy.28 = bf16[2,8,64,512]{2,0,1,3:T(2,128)(2,1)S(1)} copy(bf16[2,8,64,512]{3,2,0,1:T(8,128)(2,1)} %fusion.12) | data formatting | bytes 2097152 | tf_op jit(solution)/shard_map/convert_element_type | solution.py:45
  80.0 2.7 %reshape.46 = bf16[8,2,32768]{2,1,0:T(2,128)(2,1)} reshape(bf16[512,8,2,64]{3,2,1,0:T(2,128)(2,1)S(1)} %bitcast.85) | data formatting | bytes 2097152
  82.6 36.3 %all_to_all.54 = bf16[8,2,32768]{2,1,0:T(2,128)(2,1)} all-to-all(bf16[8,2,32768]{2,1,0:T(2,128)(2,1)} %reshape.46), channel_id=1, replica_groups=mesh['blk'=32,'sub'=8] {'sub'}, dimensions={0} | all-to-all | bytes 2097152 | tf_op jit(solution)/shard_map/all_to_all | solution.py:46
  118.9 3.1 %reshape.47 = bf16[512,8,2,64]{3,2,1,0:T(2,128)(2,1)S(1)} reshape(bf16[8,2,32768]{2,1,0:T(2,128)(2,1)} %all_to_all.54) | data formatting | bytes 2097152
  122.0 2.7 %copy.47 = bf16[2,8,64,8,64]{2,3,4,1,0:T(8,128)(2,1)} copy(bf16[2,8,64,8,64]{2,0,1,4,3:T(2,128)(2,1)S(1)} %bitcast.86) | data formatting | bytes 2097152 | tf_op jit(solution)/shard_map/all_to_all | solution.py:46
  124.7 3.2 %all_to_all.42 = bf16[2,8,512,64]{2,3,1,0:T(8,128)(2,1)S(1)} reshape(bf16[2,8,8,64,64]{3,2,4,1,0:T(8,128)(2,1)} %bitcast.87) | data formatting | bytes 2097152 | tf_op jit(solution)/shard_map/all_to_all | solution.py:46
  127.9 0.0 copy-start.2
  127.9 0.0 copy-start.3
  127.9 4.0 %fusion.25 = bf16[2,512,64]{1,2,0:T(8,128)(2,1)S(1)} fusion(bf16[2,512,512]{2,1,0:T(8,128)(2,1)S(1)} %copy-done, bf16[2,8,512,64]{2,3,1,0:T(8,128)(2,1)S(1)} %all_to_all.42, bf16[8,512,512]{2,1,0:T(8,128)(2,1)} %param.12), kind=kOutput, calls=%fused_computation.18 | convolution fusion | flops 604110848 | bytes 6422528 | tf_op jit(solution)/shard_map/jab,jbc->jac/dot_general | solution.py:50
  131.9 0.0 copy-start.1
  131.9 0.2 copy.30
  132.1 0.2 reshape.48
  132.3 11.5 %all_to_all.55 = bf16[8,2,4096]{2,1,0:T(2,128)(2,1)S(1)} all-to-all(bf16[8,2,4096]{2,1,0:T(2,128)(2,1)S(1)} %reshape.48), channel_id=1, replica_groups=mesh['blk'=32,'sub'=8] {'sub'}, dimensions={0} | all-to-all | bytes 262144 | tf_op jit(solution)/shard_map/all_to_all | solution.py:53
  143.8 0.2 reshape.49
  144.0 0.2 copy.49
  144.2 0.2 all_to_all.46
  144.4 0.0 copy-done.2
  144.4 2.3 %convolution_convert_fusion = bf16[2,64,512]{2,1,0:T(8,128)(2,1)S(1)} fusion(bf16[2,512,512]{2,1,0:T(8,128)(2,1)} %param.18, bf16[2,64,512]{2,1,0:T(8,128)(2,1)S(1)} %all_to_all.46, bf16[2,512,512]{2,1,0:T(8,128)(2,1)} %param.19, f32[2,512]{1,0:T(2,128)S(1)} %copy-done.2, f32[2,64]{1,0:T(2,128)S(1)} %copy-done.3), kind=kOutput, calls=%fused_computation.15 | convolution fusion | flops 134479872 | bytes 2363904 | tf_op jit(solution)/shard_map/jrm,jkm->jrk/dot_general | solution.py:56
  146.7 0.2 copy.32
  146.9 0.2 reshape.50
  147.1 11.5 %all_to_all.56 = bf16[8,2,4096]{2,1,0:T(2,128)(2,1)S(1)} all-to-all(bf16[8,2,4096]{2,1,0:T(2,128)(2,1)S(1)} %reshape.50), channel_id=1, replica_groups=mesh['blk'=32,'sub'=8] {'sub'}, dimensions={0} | all-to-all | bytes 262144 | tf_op jit(solution)/shard_map/all_to_all | solution.py:59
  158.6 0.2 reshape.51
  158.8 0.2 copy.48
  159.0 0.2 all_to_all.50
  159.2 1.1 convolution_bitcast_fusion
  (8 shorter events, 0.0 us)
Async XLA Ops:
  6.5 121.3 %copy-start = (bf16[2,512,512]{2,1,0:T(8,128)(2,1)S(1)}, bf16[2,512,512]{2,1,0:T(8,128)(2,1)}, u32[]{:S(2)}) copy-start(bf16[2,512,512]{2,1,0:T(8,128)(2,1)} %param.17) | copy-start | bytes 3145732
  6.5 57.1 %all-gather.2.cloned.1.call-start = ((), (), s32[]{:S(2)}) async-start(), calls=%async_computation.3 | async-start | bytes 4325376 | tf_op jit(solution)/shard_map/all_gather | solution.py:38
  127.9 16.5 %copy-start.2 = (f32[2,512]{1,0:T(2,128)S(1)}, f32[2,512]{1,0:T(2,128)}, u32[]{:S(2)}) copy-start(f32[2,512]{1,0:T(2,128)} %param.21) | copy-start | bytes 12292
  127.9 16.5 %copy-start.3 = (f32[2,64]{1,0:T(2,128)S(1)}, f32[2,64]{1,0:T(2,128)}, u32[]{:S(2)}) copy-start(f32[2,64]{1,0:T(2,128)} %param.20) | copy-start | bytes 1540
  131.9 27.3 %copy-start.1 = (bf16[2,512,512]{2,1,0:T(8,128)(2,1)S(1)}, bf16[2,512,512]{2,1,0:T(8,128)(2,1)}, u32[]{:S(2)}) copy-start(bf16[2,512,512]{2,1,0:T(8,128)(2,1)} %param.16) | copy-start | bytes 3145732
Sparse Core Ops, SparseCore 0:
  9.9 53.7 all-gather.1
where the time goes:
time: 168 us; the launch traced here: 167 us
  blocking collectives  59.2 us (35%)
  waiting for transfers between devices  55 us (33%)
  local copies, waits for them, and re-layouts  20.5 us (12%)
  matrix products  19 us (11%)
  between operations  13.6 us (8%)
    all_gather x1, waiting for transfers between devices, local(): everything = lax.all_gather(block_vec, 'blk', axis=0, tiled=True)  54.3 us
    all_to_all x1, blocking collectives, local(): lax.all_to_all(right_done, 'sub', split_axis=3, concat_axis=2, tiled=True)  36.3 us
    all_to_all x1, blocking collectives, local(): lax.all_to_all(dual_cols, 'sub', split_axis=1, concat_axis=2, tiled=True)  11.5 us
    all_to_all x1, blocking collectives, local(): lax.all_to_all(basis_rows, 'sub', split_axis=2, concat_axis=1, tiled=True)  11.5 us
    dot_general x1, matrix products, local(): jnp.einsum('ks,srn->krn', weights, everything, preferred_element_type=jnp...  6.75 us
    unnamed x14, local copies, waits for them, and re-layouts  6.67 us
    all_to_all x2, local copies, waits for them, and re-layouts, local(): lax.all_to_all(right_done, 'sub', split_axis=3, concat_axis=2, tiled=True)  5.88 us
    dot_general x1, matrix products, local(): jnp.einsum('ktrn,tmn->ktrm', pooled, right_factor, preferred_element_type...  4.8 us
  transfers between devices with their start and end apart: 1, of which 1 were waited for; matrix products, arithmetic and copies ran while one was open for 1% of the time, Pallas kernels for 0%

commit v1 on v0

--- a/solution.py
+++ b/solution.py
@@ -35,7 +35,9 @@
     ).astype(jnp.float32) * live_mask[..., None]
     source_onehot = (source[..., None] == jnp.arange(all_count)[None, None, :]).astype(jnp.float32)
     weights = jnp.einsum("gqk,gqs->ks", key_onehot, source_onehot).astype(jnp.bfloat16)
-    everything = lax.all_gather(block_vec, "blk", axis=0, tiled=True)
+    everything = jnp.concatenate(
+        lax.all_to_all(jnp.stack([block_vec] * lax.axis_size("blk")), "blk", 0, 0), axis=0
+    )
     pooled = jnp.einsum(
         "ks,srn->krn", weights, everything, preferred_element_type=jnp.float32
     ).astype(jnp.bfloat16)

time: 168 us -> 180 us (1.071)
  the two profiles are of different devices: /device:TPU:2 before, /device:TPU:8 now
where the time goes in v1:
time: 180 us; the launch traced here: 179 us
  blocking collectives  60 us (33%)
  waiting for transfers between devices  54 us (30%)
  local copies, waits for them, and re-layouts  41.7 us (23%)
  matrix products  15.3 us (8%)
  starting transfers between devices  7.72 us (4%)
    all_to_all x1, waiting for transfers between devices, local(): lax.all_to_all(jnp.stack([block_vec] * lax.axis_size('blk')), 'blk', 0, 0)  54 us
    all_to_all x1, blocking collectives, local(): lax.all_to_all(right_done, 'sub', split_axis=3, concat_axis=2, tiled=True)  37.1 us
    all_to_all x1, blocking collectives, local(): lax.all_to_all(dual_cols, 'sub', split_axis=1, concat_axis=2, tiled=True)  11.5 us
    all_to_all x1, blocking collectives, local(): lax.all_to_all(basis_rows, 'sub', split_axis=2, concat_axis=1, tiled=True)  11.5 us
    all_to_all x1, local copies, waits for them, and re-layouts, local(): lax.all_to_all(jnp.stack([block_vec] * lax.axis_size('blk')), 'blk', 0, 0)  8.76 us
    unnamed x19, local copies, waits for them, and re-layouts  7.81 us
    all_to_all x1, starting transfers between devices, local(): lax.all_to_all(jnp.stack([block_vec] * lax.axis_size('blk')), 'blk', 0, 0)  7.72 us
    reshape x1, local copies, waits for them, and re-layouts, local(): jnp.concatenate(lax.all_to_all(jnp.stack([block_vec] * lax.axis_size('blk...  7.18 us
  transfers between devices with their start and end apart: 1, of which 1 were waited for; matrix products, arithmetic and copies ran while one was open for 0% of the time, Pallas kernels for 0%

profile of v1, /device:TPU:8, one launch (start us, length us, event | category | flops | bytes accessed | tf_op | source)
XLA Modules:
  0.0 178.9 jit_solution(3544204100927510159)
XLA Ops:
  0.0 1.1 copy.26
  1.1 5.7 %stack.2 = bf16[32,2,64,512]{3,1,2,0:T(2,128)(2,1)} broadcast(bf16[2,64,512]{2,0,1:T(2,128)(2,1)S(1)} %copy.26), dimensions={1,2,3} | broadcast | bytes 4325376 | tf_op jit(solution)/shard_map/stack | solution.py:39
  6.9 7.7 %all-to-all-start = ((bf16[32,2,64,512]{3,1,2,0:T(2,128)(2,1)}), bf16[32,2,64,512]{3,1,2,0:T(2,128)(2,1)}, u32[]{:S(2)}, u32[]{:S(2)}) async-start(bf16[32,2,64,512]{3,1,2,0:T(2,128)(2,1)} %stack.2), calls=%async_computation | async-start | bytes 8388608 | tf_op jit(solution)/shard_map/all_to_all | solution.py:39
  14.6 0.2 constant_dynamic-slice_fusion
  14.8 0.1 copy.25
  14.9 0.2 dynamic-slice_reduce_fusion
  15.1 54.0 %all-to-all-done = bf16[32,2,64,512]{3,1,2,0:T(2,128)(2,1)} async-done(((bf16[32,2,64,512]{3,1,2,0:T(2,128)(2,1)}), bf16[32,2,64,512]{3,1,2,0:T(2,128)(2,1)}, u32[]{:S(2)}, u32[]{:S(2)}) %all-to-all-start) | async-done | bytes 4194336 | tf_op jit(solution)/shard_map/all_to_all | solution.py:39
  69.2 8.8 %copy.27 = bf16[32,2,64,512]{3,1,0,2:T(2,128)(2,1)} copy(bf16[32,2,64,512]{3,1,2,0:T(2,128)(2,1)} %all-to-all-done) | data formatting | bytes 8388608 | tf_op jit(solution)/shard_map/all_to_all | solution.py:39
  77.9 7.2 %reshape.44 = bf16[64,64,512]{2,0,1:T(8,128)(2,1)} reshape(bf16[32,2,64,512]{3,1,0,2:T(2,128)(2,1)} %copy.27) | data formatting | bytes 8388608 | tf_op jit(solution)/shard_map/reshape | solution.py:38
  85.1 3.0 %fusion.7 = bf16[2,8,64,512]{3,1,0,2:T(8,128)(2,1)S(1)} fusion(bf16[64,64,512]{2,0,1:T(8,128)(2,1)} %reshape.44, s32[32,2]{0,1:T(2,128)S(1)} %get-tuple-element.6, bf16[32,2]{0,1:T(2,128)(2,1)S(1)} %compare_convert_fusion, s32[32,2]{0,1:T(2,128)S(1)} %get-tuple-element.5), kind=kOutput, calls=%fused_computation.7 | convolution fusion | flops 67770368 | bytes 5243520 | tf_op jit(solution)/shard_map/ks,srn->krn/dot_general | solution.py:41
  88.1 4.8 %fusion.8 = bf16[2,8,64,512]{3,2,0,1:T(8,128)(2,1)} fusion(bf16[8,512,512]{2,1,0:T(8,128)(2,1)} %param.13, bf16[2,8,64,512]{3,1,0,2:T(8,128)(2,1)S(1)} %fusion.7), kind=kOutput, calls=%fused_computation.8 | convolution fusion | flops 537395200 | bytes 6291456 | tf_op jit(solution)/shard_map/ktrn,tmn->ktrm/dot_general | solution.py:45
  92.9 4.7 %copy.29 = bf16[2,8,64,512]{2,0,1,3:T(2,128)(2,1)S(1)} copy(bf16[2,8,64,512]{3,2,0,1:T(8,128)(2,1)} %fusion.8) | data formatting | bytes 2097152 | tf_op jit(solution)/shard_map/convert_element_type | solution.py:47
  97.7 2.7 %reshape.52 = bf16[8,2,32768]{2,1,0:T(2,128)(2,1)} reshape(bf16[512,8,2,64]{3,2,1,0:T(2,128)(2,1)S(1)} %bitcast.88) | data formatting | bytes 2097152
  100.3 37.1 %all_to_all.59 = bf16[8,2,32768]{2,1,0:T(2,128)(2,1)} all-to-all(bf16[8,2,32768]{2,1,0:T(2,128)(2,1)} %reshape.52), channel_id=1, replica_groups=mesh['blk'=32,'sub'=8] {'sub'}, dimensions={0} | all-to-all | bytes 2097152 | tf_op jit(solution)/shard_map/all_to_all | solution.py:48
  137.4 3.1 %reshape.53 = bf16[512,8,2,64]{3,2,1,0:T(2,128)(2,1)S(1)} reshape(bf16[8,2,32768]{2,1,0:T(2,128)(2,1)} %all_to_all.59) | data formatting | bytes 2097152
  140.5 2.7 %copy.42 = bf16[2,8,64,8,64]{2,3,4,1,0:T(8,128)(2,1)} copy(bf16[2,8,64,8,64]{2,0,1,4,3:T(2,128)(2,1)S(1)} %bitcast.89) | data formatting | bytes 2097152 | tf_op jit(solution)/shard_map/all_to_all | solution.py:48
  143.2 3.2 %all_to_all.46 = bf16[2,8,512,64]{2,3,1,0:T(8,128)(2,1)S(1)} reshape(bf16[2,8,8,64,64]{3,2,4,1,0:T(8,128)(2,1)} %bitcast.90) | data formatting | bytes 2097152 | tf_op jit(solution)/shard_map/all_to_all | solution.py:48
  146.5 4.0 %fusion.18 = bf16[2,512,64]{1,2,0:T(8,128)(2,1)S(1)} fusion(bf16[2,512,512]{2,1,0:T(8,128)(2,1)S(1)} %copy-done, bf16[2,8,512,64]{2,3,1,0:T(8,128)(2,1)S(1)} %all_to_all.46, bf16[8,512,512]{2,1,0:T(8,128)(2,1)} %param.12), kind=kOutput, calls=%fused_computation.16 | convolution fusion | flops 604110848 | bytes 6422528 | tf_op jit(solution)/shard_map/jab,jbc->jac/dot_general | solution.py:52
  150.5 0.2 copy.31
  150.6 0.2 reshape.54
  150.9 11.5 %all_to_all.60 = bf16[8,2,4096]{2,1,0:T(2,128)(2,1)S(1)} all-to-all(bf16[8,2,4096]{2,1,0:T(2,128)(2,1)S(1)} %reshape.54), channel_id=1, replica_groups=mesh['blk'=32,'sub'=8] {'sub'}, dimensions={0} | all-to-all | bytes 262144 | tf_op jit(solution)/shard_map/all_to_all | solution.py:55
  162.4 0.2 reshape.55
  162.6 0.2 copy.44
  162.8 0.2 all_to_all.50
  163.0 2.3 %convolution_convert_fusion.1 = bf16[2,64,512]{2,1,0:T(8,128)(2,1)S(1)} fusion(bf16[2,512,512]{2,1,0:T(8,128)(2,1)} %param.18, bf16[2,64,512]{2,1,0:T(8,128)(2,1)S(1)} %all_to_all.50, bf16[2,512,512]{2,1,0:T(8,128)(2,1)} %param.19, f32[2,512]{1,0:T(2,128)S(1)} %copy-done.4, f32[2,64]{1,0:T(2,128)S(1)} %copy-done.5), kind=kOutput, calls=%fused_computation.13 | convolution fusion | flops 134479872 | bytes 2363904 | tf_op jit(solution)/shard_map/jrm,jkm->jrk/dot_general | solution.py:58
  165.3 0.2 copy.33
  165.5 0.2 reshape.56
  165.7 11.5 %all_to_all.61 = bf16[8,2,4096]{2,1,0:T(2,128)(2,1)S(1)} all-to-all(bf16[8,2,4096]{2,1,0:T(2,128)(2,1)S(1)} %reshape.56), channel_id=1, replica_groups=mesh['blk'=32,'sub'=8] {'sub'}, dimensions={0} | all-to-all | bytes 262144 | tf_op jit(solution)/shard_map/all_to_all | solution.py:61
  177.2 0.2 reshape.57
  177.4 0.2 copy.43
  177.6 0.2 all_to_all.54
  177.8 1.1 convolution_bitcast_fusion
  (15 shorter events, 0.0 us)
Async XLA Ops:
  0.0 146.4 %copy-start = (bf16[2,512,512]{2,1,0:T(8,128)(2,1)S(1)}, bf16[2,512,512]{2,1,0:T(8,128)(2,1)}, u32[]{:S(2)}) copy-start(bf16[2,512,512]{2,1,0:T(8,128)(2,1)} %param.17) | copy-start | bytes 3145732
  6.9 7.7 %copy-start.2 = (s32[32,32,2,3]{1,2,3,0:T(2,128)S(1)}, s32[32,32,2,3]{1,2,3,0:T(2,128)}, u32[]{:S(2)}) copy-start(s32[32,32,2,3]{1,2,3,0:T(2,128)} %param.14) | copy-start | bytes 73732
  6.9 8.0 %copy-start.3 = (s32[32,32]{1,0:T(8,128)S(1)}, s32[32,32]{1,0:T(8,128)}, u32[]{:S(2)}) copy-start(s32[32,32]{1,0:T(8,128)} %param.15) | copy-start | bytes 12292
  6.9 62.3 %all-to-all-start = ((bf16[32,2,64,512]{3,1,2,0:T(2,128)(2,1)}), bf16[32,2,64,512]{3,1,2,0:T(2,128)(2,1)}, u32[]{:S(2)}, u32[]{:S(2)}) async-start(bf16[32,2,64,512]{3,1,2,0:T(2,128)(2,1)} %stack.2), calls=%async_computation | async-start | bytes 8388608 | tf_op jit(solution)/shard_map/all_to_all | solution.py:39
  146.5 16.5 %copy-start.4 = (f32[2,512]{1,0:T(2,128)S(1)}, f32[2,512]{1,0:T(2,128)}, u32[]{:S(2)}) copy-start(f32[2,512]{1,0:T(2,128)} %param.21) | copy-start | bytes 12292
  146.5 16.5 %copy-start.5 = (f32[2,64]{1,0:T(2,128)S(1)}, f32[2,64]{1,0:T(2,128)}, u32[]{:S(2)}) copy-start(f32[2,64]{1,0:T(2,128)} %param.20) | copy-start | bytes 1540
  150.5 27.3 %copy-start.1 = (bf16[2,512,512]{2,1,0:T(8,128)(2,1)S(1)}, bf16[2,512,512]{2,1,0:T(8,128)(2,1)}, u32[]{:S(2)}) copy-start(bf16[2,512,512]{2,1,0:T(8,128)(2,1)} %param.16) | copy-start | bytes 3145732
